TPU v7x, 256 devices: a whole 4x4x8 slice. The times are simulated.
256 devices in a mesh: pos: 16 (over x_hi, z), exp: 16 (over y, x_lo, core).
Axes of the slice: x: 4 (x_hi: 2, x_lo: 2; x = x_hi * 2 + x_lo), y: 4, z: 8, core: 2. Of those that a mesh axis runs over, the one named last changes fastest.
Arguments:
- patches: bfloat16 [65536, 4, 256], P(('pos', 'exp')), may hold values from -6 to 6
- conv_weight: bfloat16 [3, 256, 2048], replicated, may hold values from -0.21875 to 0.21875
- phi: bfloat16 [2048, 128], replicated, may hold values from -40 to 40, as said below
- w_in: bfloat16 [16, 2048, 8192], P('exp', None, 'pos'), may hold values from -0.125 to 0.125
- w_out: bfloat16 [16, 8192, 2048], P('exp', 'pos'), may hold values from -0.0625 to 0.0625
Outputs:
- mixed: bfloat16 [65536, 4, 2048], P(('pos', 'exp'))
Inputs may be any that keep to these rules, and one draw needn't show every extreme that they name: phi is real-valued.
All inputs are finite; a program needn't handle non-finite values.
Results may differ from a plain program's by a relative error of at most 0.019.
The roundings to bfloat16 on the way count: a program that leaves them out, or rounds other values in their place, can miss the bound.
Values may be sent and summed in bfloat16 or wider, within the bound.
No kernel may reach another device: no remote copies, remote signals or barrier semaphores. Data moves between devices by JAX's collectives and lax.ppermute only.
A program may use at most 128 MiB of HBM per device.

v0:
```python
import jax
import jax.numpy as jnp
from jax import lax
from jax.sharding import PartitionSpec as P

D = 2048
SLOTS_PER = 8


def with_halo(array, sides, width):
    for axis, dim in sides:
        count, length = (lax.axis_size(axis), array.shape[dim])
        up = [(i, (i + 1) % count) for i in range(count - 1)]
        down = [(j, i) for i, j in up]
        last = lax.slice_in_dim(array, length - width, length, axis=dim)
        initial = lax.slice_in_dim(array, 0, width, axis=dim)
        before = lax.ppermute(last, axis, up)
        after = lax.ppermute(initial, axis, down)
        array = jnp.concatenate([before, array, after], axis=dim)
    return array


def per_device(patches, conv_weight, phi, w_in, w_out):
    channels, periods, samples = patches.shape
    padded = with_halo(patches, ((("pos", "exp"), 0),), 1)
    running = jnp.zeros((channels * periods, D), jnp.float32)
    for offset in range(3):
        window = padded[offset : offset + channels].reshape(channels * periods, samples)
        running = running + jnp.dot(window, conv_weight[offset], preferred_element_type=jnp.float32)
    flat = running.astype(jnp.bfloat16)
    logits = jnp.dot(flat, phi, preferred_element_type=jnp.float32)
    local_peak = jnp.max(logits, axis=0)
    column_peak = lax.pmax(local_peak, ("pos", "exp"))
    raw_weights = jnp.exp(logits - column_peak)
    column_total = lax.psum(jnp.sum(raw_weights, axis=0), ("pos", "exp"))
    dispatch = (raw_weights / column_total).astype(jnp.bfloat16)
    group = lax.axis_index("exp")
    every_slot = lax.dot_general(
        dispatch, flat, (((0,), (0,)), ((), ())), preferred_element_type=jnp.float32
    )
    summed = lax.psum(every_slot, ("pos", "exp"))
    owned = lax.dynamic_slice_in_dim(summed, group * SLOTS_PER, SLOTS_PER, 0)
    slot_in = owned.astype(jnp.bfloat16)
    hidden = jax.nn.gelu(
        jnp.dot(slot_in, w_in[0], preferred_element_type=jnp.float32), approximate=True
    ).astype(jnp.bfloat16)
    expert_term = jnp.dot(hidden, w_out[0], preferred_element_type=jnp.float32)
    slot_out = lax.psum(expert_term, "pos").astype(jnp.bfloat16)
    row_peak = jnp.max(logits, axis=1, keepdims=True)
    row_weights = jnp.exp(logits - row_peak)
    combine = (row_weights / jnp.sum(row_weights, axis=1, keepdims=True)).astype(jnp.bfloat16)
    mixed = jnp.dot(
        combine,
        lax.all_gather(slot_out, "exp", axis=0, tiled=True),
        preferred_element_type=jnp.float32,
    )
    return mixed.astype(jnp.bfloat16).reshape(channels, periods, D)


def solution(mesh):
    in_specs = (
        P(("pos", "exp"), None, None),
        P(),
        P(),
        P("exp", None, "pos"),
        P("exp", "pos", None),
    )
    out_specs = P(("pos", "exp"), None, None)
    return jax.shard_map(
        per_device, mesh=mesh, in_specs=in_specs, out_specs=out_specs, check_vma=False
    )
```

profile of v0, /device:TPU:1, one launch (start us, length us, event | category | flops | bytes accessed | tf_op | source)
XLA Modules:
  0.0 376.0 jit_solution(2195007920341952127)
XLA Ops:
  0.0 0.0 copy-start
  0.0 0.9 fusion.47
  0.9 4.5 %collective-permute-start = (bf16[1,4,256]{2,1,0:T(4,128)(2,1)S(1)}, bf16[1,4,256]{2,1,0:T(4,128)(2,1)S(1)}, u32[]{:S(2)}, u32[]{:S(2)}) collective-permute-start(bf16[1,4,256]{2,1,0:T(4,128)(2,1)S(1)} %get-tuple-element.12), channel_id=1, source_target_pairs={{0,1},{1,2},{2,3},{3,4},{4,5},{5,6},{6,7},{7,8},{8,9},{9,10},{10,1... | collective-permute-start | bytes 6152 | tf_op jit(solution)/shard_map/ppermute | solution.py:17
  5.3 1.9 collective-permute-start.1
  7.3 1.2 reshape.17
  8.4 0.0 copy-start.2
  8.5 5.8 %fusion.8 = f32[1024,2048]{1,0:T(8,128)} fusion(bf16[1024,256]{1,0:T(8,128)(2,1)S(1)} %reshape.17, bf16[3,256,2048]{2,1,0:T(8,128)(2,1)} %param.6), kind=kOutput, calls=%fused_computation.8 | convolution fusion | flops 1073741824 | bytes 9961472 | tf_op jit(solution)/shard_map/dot_general | solution.py:29
  14.2 0.0 collective-permute-done
  14.2 0.0 collective-permute-done.1
  14.2 0.0 copy-done.2
  14.2 1.3 pad_maximum_fusion
  15.6 1.2 reshape.16
  16.7 0.0 copy-start.3
  16.8 5.8 %fusion.10 = f32[1024,2048]{1,0:T(8,128)} fusion(bf16[1024,256]{1,0:T(8,128)(2,1)S(1)} %reshape.16, bf16[3,256,2048]{2,1,0:T(8,128)(2,1)} %param.6), kind=kOutput, calls=%fused_computation.10 | convolution fusion | flops 1073741824 | bytes 9961472 | tf_op jit(solution)/shard_map/dot_general | solution.py:29
  22.5 0.0 copy-done.3
  22.5 0.1 reshape.18
  22.6 0.0 copy-start.4
  22.7 7.4 %add_convert_fusion = bf16[1024,2048]{1,0:T(8,128)(2,1)S(1)} fusion(f32[1024,2048]{1,0:T(8,128)} %fusion.10, f32[1024,2048]{1,0:T(8,128)} %fusion.8, bf16[1024,256]{1,0:T(8,128)(2,1)S(1)} %reshape.18, bf16[3,256,2048]{2,1,0:T(8,128)(2,1)} %param.6), kind=kOutput, calls=%fused_computation | convolution fusion | flops 1080033280 | bytes 22544384 | tf_op jit(solution)/shard_map/dot_general | solution.py:29
  30.0 0.0 copy-start.1
  30.1 2.0 copy-done.1
  32.1 0.0 copy-done.4
  32.1 1.3 fusion.46
  33.4 80.7 %pmax.7 = f32[128]{0:T(128)S(1)} all-reduce(f32[128]{0:T(128)S(1)} %get-tuple-element.8), channel_id=1, replica_groups=mesh['pos'=16,'exp'=16] {'pos','exp'}, use_global_device_ids=true, to_apply=%region_3.0 | all-reduce | flops 128 | bytes 1024 | tf_op jit(solution)/shard_map/pmax | solution.py:33
  114.1 0.4 fusion.15
  114.5 72.9 %psum.21 = f32[128]{0:T(128)S(1)} all-reduce(f32[128]{0:T(128)S(1)} %get-tuple-element.6), channel_id=1, replica_groups=mesh['pos'=16,'exp'=16] {'pos','exp'}, use_global_device_ids=true, to_apply=%region_5.0 | all-reduce | flops 128 | bytes 1024 | tf_op jit(solution)/shard_map/psum | solution.py:35
  187.4 3.9 %fusion.17 = f32[128,2048]{1,0:T(8,128)} fusion(bf16[1024,2048]{1,0:T(8,128)(2,1)} %copy-done.1, f32[1024,128]{1,0:T(8,128)S(1)} %get-tuple-element.13, f32[128]{0:T(128)S(1)} %psum.21, f32[128]{0:T(128)S(1)} %pmax.7), kind=kOutput, calls=%fused_computation.23 | convolution fusion | flops 537264128 | bytes 5768192 | tf_op jit(solution)/shard_map/dot_general | solution.py:38
  191.3 78.0 %all-reduce.1 = bf16[128,2048]{1,0:T(8,128)(2,1)S(1)} all-reduce(f32[128,2048]{1,0:T(8,128)} %fusion.17), channel_id=1, replica_groups=mesh['pos'=16,'exp'=16] {'pos','exp'}, use_global_device_ids=true, to_apply=%region_6.0 | all-reduce | flops 262144 | bytes 1572864 | tf_op jit(solution)/shard_map/psum | solution.py:41
  269.4 0.0 copy-done
  269.4 2.3 fusion
  271.7 62.1 %psum.23 = bf16[8,2048]{1,0:T(8,128)(2,1)S(1)} all-reduce(f32[8,2048]{1,0:T(8,128)S(1)} %fusion), channel_id=1, replica_groups=mesh['pos'=16,'exp'=16] {'pos'}, use_global_device_ids=true, to_apply=%region_7.0 | all-reduce | flops 16384 | bytes 98304 | tf_op jit(solution)/shard_map/psum | solution.py:48
  333.8 31.7 %all_gather.3 = bf16[128,2048]{1,0:T(8,128)(2,1)S(1)} all-gather(bf16[8,2048]{1,0:T(8,128)(2,1)S(1)} %psum.23), channel_id=1, replica_groups=mesh['pos'=16,'exp'=16] {'exp'}, dimensions={0}, use_global_device_ids=true | all-gather | bytes 557056 | tf_op jit(solution)/shard_map/all_gather | solution.py:54
  365.6 3.3 convolution_convert_fusion
  368.8 7.2 %reshape.19 = bf16[256,4,2048]{2,1,0:T(4,128)(2,1)} reshape(bf16[1024,2048]{1,0:T(8,128)(2,1)} %convolution_convert_fusion) | data formatting | bytes 8388608 | tf_op jit(solution)/shard_map/reshape | solution.py:57
Async XLA Ops:
  0.0 269.4 %copy-start = (bf16[1,512,2048]{2,1,0:T(8,128)(2,1)S(1)}, bf16[1,512,2048]{2,1,0:T(8,128)(2,1)}, u32[]{:S(2)}) copy-start(bf16[1,512,2048]{2,1,0:T(8,128)(2,1)} %param.9) | copy-start | bytes 6291460
  0.9 13.4 %collective-permute-start = (bf16[1,4,256]{2,1,0:T(4,128)(2,1)S(1)}, bf16[1,4,256]{2,1,0:T(4,128)(2,1)S(1)}, u32[]{:S(2)}, u32[]{:S(2)}) collective-permute-start(bf16[1,4,256]{2,1,0:T(4,128)(2,1)S(1)} %get-tuple-element.12), channel_id=1, source_target_pairs={{0,1},{1,2},{2,3},{3,4},{4,5},{5,6},{6,7},{7,8},{8,9},{9,10},{10,1... | collective-permute-start | bytes 6152 | tf_op jit(solution)/shard_map/ppermute | solution.py:17
  5.3 8.9 %collective-permute-start.1 = (bf16[1,4,256]{2,1,0:T(4,128)(2,1)S(1)}, bf16[1,4,256]{2,1,0:T(4,128)(2,1)S(1)}, u32[]{:S(2)}, u32[]{:S(2)}) collective-permute-start(bf16[1,4,256]{2,1,0:T(4,128)(2,1)S(1)} %get-tuple-element.11), channel_id=1, source_target_pairs={{1,0},{2,1},{3,2},{4,3},{5,4},{6,5},{7,6},{8,7},{9,8},{10,9},{11,1... | collective-permute-start | bytes 6152 | tf_op jit(solution)/shard_map/ppermute | solution.py:18
  8.4 5.8 %copy-start.2 = (bf16[256,4,256]{2,1,0:T(4,128)(2,1)S(1)}, bf16[256,4,256]{2,1,0:T(4,128)(2,1)}, u32[]{:S(2)}) copy-start(bf16[256,4,256]{2,1,0:T(4,128)(2,1)} %param.5) | copy-start | bytes 1572868
  16.7 5.8 %copy-start.3 = (bf16[256,4,256]{2,1,0:T(4,128)(2,1)S(1)}, bf16[256,4,256]{2,1,0:T(4,128)(2,1)}, u32[]{:S(2)}) copy-start(bf16[256,4,256]{2,1,0:T(4,128)(2,1)} %get-tuple-element.9) | copy-start | bytes 1572868
  22.6 9.4 %copy-start.4 = (bf16[2048,128]{1,0:T(8,128)(2,1)S(1)}, bf16[2048,128]{1,0:T(8,128)(2,1)}, u32[]{:S(2)}) copy-start(bf16[2048,128]{1,0:T(8,128)(2,1)} %param.7) | copy-start | bytes 1572868
  30.0 2.0 copy-start.1
where the time goes:
time: 377 us; the launch traced here: 376 us
  blocking collectives  326 us (86%)
  matrix products  29.8 us (8%)
  local copies, waits for them, and re-layouts  12.5 us (3%)
  starting transfers between devices  6.41 us (2%)
    pmax x1, blocking collectives, per_device(): column_peak = lax.pmax(local_peak, ('pos', 'exp'))  80.7 us
    psum x1, blocking collectives, per_device(): summed = lax.psum(every_slot, ('pos', 'exp'))  78 us
    psum x1, blocking collectives, per_device(): column_total = lax.psum(jnp.sum(raw_weights, axis=0), ('pos', 'exp'))  72.9 us
    psum x1, blocking collectives, per_device(): slot_out = lax.psum(expert_term, 'pos').astype(jnp.bfloat16)  62.1 us
    all_gather x1, blocking collectives, per_device(): lax.all_gather(slot_out, 'exp', axis=0, tiled=True)  31.7 us
    dot_general x3, matrix products, per_device(): jnp.dot(window, conv_weight[offset], preferred_element_type=jnp.float32)  18.9 us
  transfers between devices with their start and end apart: 2, of which 0 were waited for; matrix products, arithmetic and copies ran while one was open for 2% of the time, Pallas kernels for 0%

commit v1 on v0

--- a/solution.py
+++ b/solution.py
@@ -32,7 +32,7 @@
     local_peak = jnp.max(logits, axis=0)
     column_peak = lax.pmax(local_peak, ("pos", "exp"))
     raw_weights = jnp.exp(logits - column_peak)
-    column_total = lax.psum(jnp.sum(raw_weights, axis=0), ("pos", "exp"))
+    column_total = jnp.sum(lax.all_gather(jnp.sum(raw_weights, axis=0), ("pos", "exp")), axis=0)
     dispatch = (raw_weights / column_total).astype(jnp.bfloat16)
     group = lax.axis_index("exp")
     every_slot = lax.dot_general(

time: 377 us -> 643 us (1.71)
  blocking collectives: 326 us -> 592 us
    all_gather x0 -> x1, blocking collectives: none -> 341 us  [per_device(): lax.all_gather(jnp.sum(raw_weights, axis=0), ('pos', 'exp'))]
    psum x1 -> x0, blocking collectives: 72.9 us -> none  [per_device(): column_total = lax.psum(jnp.sum(raw_weights, axis=0), ('pos', 'exp'))]
  transfers between devices with their start and end apart: 2 -> 2, of which waited for: 0 -> 0; matrix products, arithmetic and copies ran while one was open for 2% -> 1% of each run, Pallas kernels for 0% -> 0%
where the time goes in v1:
time: 643 us
  blocking collectives  592 us (92%)
  matrix products  29.7 us (5%)
  local copies, waits for them, and re-layouts  12.5 us (2%)
    all_gather x1, blocking collectives, per_device(): lax.all_gather(jnp.sum(raw_weights, axis=0), ('pos', 'exp'))  341 us
    pmax x1, blocking collectives, per_device(): column_peak = lax.pmax(local_peak, ('pos', 'exp'))  80.7 us
    psum x1, blocking collectives, per_device(): summed = lax.psum(every_slot, ('pos', 'exp'))  75.9 us
    psum x1, blocking collectives, per_device(): slot_out = lax.psum(expert_term, 'pos').astype(jnp.bfloat16)  61.8 us
    all_gather x1, blocking collectives, per_device(): lax.all_gather(slot_out, 'exp', axis=0, tiled=True)  32.4 us
    dot_general x3, matrix products, per_device(): jnp.dot(window, conv_weight[offset], preferred_element_type=jnp.float32)  18.9 us
  transfers between devices with their start and end apart: 2, of which 0 were waited for; matrix products, arithmetic and copies ran while one was open for 1% of the time, Pallas kernels for 0%

profile of v1, /device:TPU:1, one launch (start us, length us, event | category | flops | bytes accessed | tf_op | source)
XLA Modules:
  0.0 642.8 jit_solution(12792812096105564002)
XLA Ops:
  0.0 0.0 copy-start
  0.0 0.9 fusion.47
  0.9 4.5 collective-permute-start
  5.3 1.9 collective-permute-start.1
  7.3 1.2 reshape.17
  8.4 0.0 copy-start.2
  8.5 5.8 fusion.8
  14.2 0.0 collective-permute-done
  14.2 0.0 collective-permute-done.1
  14.2 0.0 copy-done.2
  14.2 1.3 pad_maximum_fusion
  15.6 1.2 reshape.16
  16.7 0.0 copy-start.3
  16.8 5.8 fusion.10
  22.5 0.0 copy-done.3
  22.5 0.1 reshape.18
  22.6 0.0 copy-start.4
  22.7 7.4 %add_convert_fusion = bf16[1024,2048]{1,0:T(8,128)(2,1)S(1)} fusion(f32[1024,2048]{1,0:T(8,128)} %fusion.10, f32[1024,2048]{1,0:T(8,128)} %fusion.8, bf16[1024,256]{1,0:T(8,128)(2,1)S(1)} %reshape.18, bf16[3,256,2048]{2,1,0:T(8,128)(2,1)} %param.6), kind=kOutput, calls=%fused_computation | convolution fusion | flops 1080033280 | bytes 22544384 | tf_op jit(solution)/shard_map/dot_general | solution.py:29
  30.0 0.0 copy-start.1
  30.1 2.0 copy-done.1
  32.1 0.0 copy-done.4
  32.1 1.3 fusion.46
  33.4 80.7 %pmax.7 = f32[128]{0:T(128)S(1)} all-reduce(f32[128]{0:T(128)S(1)} %get-tuple-element.8), channel_id=1, replica_groups=mesh['pos'=16,'exp'=16] {'pos','exp'}, use_global_device_ids=true, to_apply=%region_3.0 | all-reduce | flops 128 | bytes 1024 | tf_op jit(solution)/shard_map/pmax | solution.py:33
  114.1 0.4 fusion.15
  114.5 341.2 %all-gather.1 = f32[256,1,128]{2,1,0:T(1,128)S(1)} all-gather(f32[1,1,128]{2,1,0:T(1,128)S(1)} %bitcast.31), channel_id=2, replica_groups=mesh['pos'=16,'exp'=16] {'pos','exp'}, dimensions={0}, use_global_device_ids=true | all-gather | bytes 131584 | tf_op jit(solution)/shard_map/all_gather | solution.py:35
  455.7 0.3 reduce_sum.29
  455.9 3.9 fusion.17
  459.9 75.9 %all-reduce.1 = bf16[128,2048]{1,0:T(8,128)(2,1)S(1)} all-reduce(f32[128,2048]{1,0:T(8,128)} %fusion.17), channel_id=1, replica_groups=mesh['pos'=16,'exp'=16] {'pos','exp'}, use_global_device_ids=true, to_apply=%region_6.0 | all-reduce | flops 262144 | bytes 1572864 | tf_op jit(solution)/shard_map/psum | solution.py:41
  535.8 0.0 copy-done
  535.8 2.3 fusion
  538.1 61.8 %psum.15 = bf16[8,2048]{1,0:T(8,128)(2,1)S(1)} all-reduce(f32[8,2048]{1,0:T(8,128)S(1)} %fusion), channel_id=1, replica_groups=mesh['pos'=16,'exp'=16] {'pos'}, use_global_device_ids=true, to_apply=%region_7.0 | all-reduce | flops 16384 | bytes 98304 | tf_op jit(solution)/shard_map/psum | solution.py:48
  600.0 32.4 %all_gather.11 = bf16[128,2048]{1,0:T(8,128)(2,1)S(1)} all-gather(bf16[8,2048]{1,0:T(8,128)(2,1)S(1)} %psum.15), channel_id=1, replica_groups=mesh['pos'=16,'exp'=16] {'exp'}, dimensions={0}, use_global_device_ids=true | all-gather | bytes 557056 | tf_op jit(solution)/shard_map/all_gather | solution.py:54
  632.3 3.2 convolution_convert_fusion
  635.6 7.2 %reshape.19 = bf16[256,4,2048]{2,1,0:T(4,128)(2,1)} reshape(bf16[1024,2048]{1,0:T(8,128)(2,1)} %convolution_convert_fusion) | data formatting | bytes 8388608 | tf_op jit(solution)/shard_map/reshape | solution.py:57
Async XLA Ops:
  0.0 535.8 %copy-start = (bf16[1,512,2048]{2,1,0:T(8,128)(2,1)S(1)}, bf16[1,512,2048]{2,1,0:T(8,128)(2,1)}, u32[]{:S(2)}) copy-start(bf16[1,512,2048]{2,1,0:T(8,128)(2,1)} %param.9) | copy-start | bytes 6291460
  0.9 13.4 %collective-permute-start = (bf16[1,4,256]{2,1,0:T(4,128)(2,1)S(1)}, bf16[1,4,256]{2,1,0:T(4,128)(2,1)S(1)}, u32[]{:S(2)}, u32[]{:S(2)}) collective-permute-start(bf16[1,4,256]{2,1,0:T(4,128)(2,1)S(1)} %get-tuple-element.12), channel_id=1, source_target_pairs={{0,1},{1,2},{2,3},{3,4},{4,5},{5,6},{6,7},{7,8},{8,9},{9,10},{10,1... | collective-permute-start | bytes 6152 | tf_op jit(solution)/shard_map/ppermute | solution.py:17
  5.3 8.9 %collective-permute-start.1 = (bf16[1,4,256]{2,1,0:T(4,128)(2,1)S(1)}, bf16[1,4,256]{2,1,0:T(4,128)(2,1)S(1)}, u32[]{:S(2)}, u32[]{:S(2)}) collective-permute-start(bf16[1,4,256]{2,1,0:T(4,128)(2,1)S(1)} %get-tuple-element.11), channel_id=1, source_target_pairs={{1,0},{2,1},{3,2},{4,3},{5,4},{6,5},{7,6},{8,7},{9,8},{10,9},{11,1... | collective-permute-start | bytes 6152 | tf_op jit(solution)/shard_map/ppermute | solution.py:18
  8.4 5.8 copy-start.2
  16.7 5.8 copy-start.3
  22.6 9.4 %copy-start.4 = (bf16[2048,128]{1,0:T(8,128)(2,1)S(1)}, bf16[2048,128]{1,0:T(8,128)(2,1)}, u32[]{:S(2)}) copy-start(bf16[2048,128]{1,0:T(8,128)(2,1)} %param.7) | copy-start | bytes 1572868
  30.0 2.0 copy-start.1
